TPU v7x, 32 devices: a whole 2x2x4 slice. The times are simulated.
32 devices in a mesh: uv: 8 (over y, x, core), chan: 4 (over z).
Axes of the slice: x: 2, y: 2, z: 4, core: 2. Of those that a mesh axis runs over, the one named last changes fastest.
Arguments:
- vis: bfloat16 [98304, 2, 1024], P('uv', None, 'chan'), may hold values from -6 to 6
- row_cell: int32 [98304], P('uv'), may hold values from 0 to 127
- tap_weight: bfloat16 [8, 98304], P(None, 'uv'), may hold values from 0.029907227 to 0.29882812
- tap_offset: int32 [8], replicated, may hold values from -32 to 32
- block_tile: int32 [768], P('uv'), may hold values from 0 to 79, as said below
- tile_owner: int32 [80], replicated, may hold values from 0 to 7, as said below
- galaxy: bfloat16 [152, 128, 2048], P('uv', 'chan'), may hold values from -6 to 6
Outputs:
- delay_cube: bfloat16 [152, 128, 2048], P('uv', 'chan')
- cross_power: float32 [152, 1024], P('uv')
Inputs may be any that keep to these rules, and one draw needn't show every extreme that they name: `tile_owner`: each of the 8 owners holds 1 to 19 tiles, and some owner exactly 19. `block_tile`: of the 96 row blocks of one index of uv, at most 22 lie in tiles of one owner, and exactly 22 lie in the tiles of some owner.
All inputs are finite; a program needn't handle non-finite values.
Results may differ from a plain program's by a relative error of at most 0.0059.
Values may be sent and summed in bfloat16 or wider, within the bound.
No kernel may reach another device: no remote copies, remote signals or barrier semaphores. Data moves between devices by JAX's collectives and lax.ppermute only.
A program may use at most 128 MiB of HBM per device.

v0:
```python
import math
import jax
import jax.numpy as jnp
from jax import lax
from jax.sharding import PartitionSpec as P

CH = 1024
BR = 128
TC = 128
KT = 8
TILES_DEV = 10


def tile_ranks(tile_owner, owners):
    onehot = (tile_owner[:, None] == jnp.arange(owners, dtype=jnp.int32)[None, :]).astype(jnp.int32)
    before = jnp.cumsum(onehot, axis=0) - onehot
    return jnp.sum(before * onehot, axis=1)


def kernel_matrix(cells, weights, tap_offset):
    positions = jnp.arange(TC, dtype=jnp.int32)
    total = jnp.zeros(cells.shape[:-1] + (TC, cells.shape[-1]), jnp.float32)
    for k in range(KT):
        target = cells + tap_offset[k]
        hit = target[..., None, :] == positions[:, None]
        total = total + jnp.where(
            hit, weights[..., k, :].astype(jnp.float32)[..., None, :], jnp.float32(0.0)
        )
    return total.astype(jnp.bfloat16)


def delay_table():
    freq = jnp.arange(CH, dtype=jnp.int32)
    phase = (freq[:, None] * freq[None, :] % CH).astype(jnp.float32) * jnp.float32(
        2.0 * math.pi / CH
    )
    cosine = jnp.cos(phase)
    sine = jnp.sin(phase)
    x = freq.astype(jnp.float32) * jnp.float32(2.0 * math.pi / CH)
    taper = 0.35875 - 0.48829 * jnp.cos(x) + 0.14128 * jnp.cos(2.0 * x) - 0.01168 * jnp.cos(3.0 * x)
    scale = (taper / jnp.float32(math.sqrt(CH)))[:, None]
    upper = jnp.concatenate([cosine * scale, -sine * scale], axis=1)
    lower = jnp.concatenate([sine * scale, cosine * scale], axis=1)
    return jnp.concatenate([upper, lower], axis=0).astype(jnp.bfloat16)


def body(vis, row_cell, tap_weight, tap_offset, block_tile, tile_owner, galaxy):
    n_owners = lax.axis_size("uv")
    nblocks = block_tile.shape[0]
    mean_load = nblocks // n_owners
    capacity = mean_load + (TILES_DEV - 1) * mean_load // TILES_DEV
    slots_dev = 2 * TILES_DEV - 1
    chan_dev = vis.shape[2]
    buffer_size = n_owners * capacity
    rank_of_tile = tile_ranks(tile_owner, n_owners)
    target_owner = tile_owner[block_tile]
    owner_hot = (target_owner[:, None] == jnp.arange(n_owners, dtype=jnp.int32)[None, :]).astype(
        jnp.int32
    )
    earlier = jnp.cumsum(owner_hot, axis=0) - owner_hot
    place = target_owner * capacity + jnp.sum(earlier * owner_hot, axis=1)
    blocks = vis.reshape(nblocks, BR, 2 * chan_dev)
    cells = row_cell.reshape(nblocks, BR)
    weights = jnp.transpose(tap_weight.reshape(KT, nblocks, BR), (1, 0, 2))
    sent_vis = jnp.zeros((buffer_size, BR, 2 * chan_dev), jnp.bfloat16).at[place].set(blocks)
    sent_tile = jnp.full((buffer_size,), -1, jnp.int32).at[place].set(block_tile)
    sent_cells = jnp.zeros((buffer_size, BR), jnp.int32).at[place].set(cells)
    sent_weights = jnp.zeros((buffer_size, KT, BR), jnp.bfloat16).at[place].set(weights)
    got_vis, got_tile, got_cells, got_weights = (
        lax.all_to_all(sent_vis, "uv", split_axis=0, concat_axis=0, tiled=True),
        lax.all_to_all(sent_tile, "uv", split_axis=0, concat_axis=0, tiled=True),
        lax.all_to_all(sent_cells, "uv", split_axis=0, concat_axis=0, tiled=True),
        lax.all_to_all(sent_weights, "uv", split_axis=0, concat_axis=0, tiled=True),
    )
    got_matrix = kernel_matrix(got_cells, got_weights, tap_offset)
    contrib = jnp.einsum("bcr,brf->bcf", got_matrix, got_vis, preferred_element_type=jnp.float32)
    slot = jnp.where(got_tile >= 0, rank_of_tile[jnp.maximum(got_tile, 0)], -1)
    pick = (slot[:, None] == jnp.arange(slots_dev, dtype=jnp.int32)[None, :]).astype(jnp.float32)
    grid = jnp.einsum("bs,bcf->scf", pick, contrib, precision=lax.Precision.HIGHEST)
    gridded = grid.astype(jnp.bfloat16).reshape(slots_dev, TC, 2, chan_dev)
    table = delay_table()
    piece = lax.all_to_all(gridded, "chan", split_axis=1, concat_axis=3, tiled=True)
    count = piece.shape[0]
    cells_part = piece.shape[1]
    flat = piece.reshape(count * cells_part, 2 * CH)
    out = jnp.dot(flat, table, preferred_element_type=jnp.float32)
    delay = out.reshape(count, cells_part, 2 * CH)
    galaxy_f = galaxy.astype(jnp.float32)
    product = delay[..., :CH] * galaxy_f[..., :CH] + delay[..., CH:] * galaxy_f[..., CH:]
    local_power = jnp.sum(product, axis=1)
    power = lax.psum(local_power, "chan") / jnp.float32(math.sqrt(TC))
    return (delay.astype(jnp.bfloat16), power)


def solution(mesh):
    return jax.shard_map(
        body,
        mesh=mesh,
        in_specs=(
            P("uv", None, "chan"),
            P("uv"),
            P(None, "uv"),
            P(),
            P("uv"),
            P(),
            P("uv", "chan", None),
        ),
        out_specs=(P("uv", "chan", None), P("uv", None)),
        check_vma=False,
    )
```

profile of v0, /device:TPU:0, one launch (start us, length us, event | category | flops | bytes accessed | tf_op | source)
XLA Modules:
  0.0 569.6 jit_solution(16998166635543470072)
XLA Ops:
  7.9 1.6 gather_fusion
  9.9 1.0 scatter_custom_fusion
  10.9 0.7 all_to_all.29
  11.6 5.2 all-to-all-start
  16.8 0.8 scatter_custom_fusion.1
  18.2 3.1 all-to-all-done
  21.4 3.4 all-to-all-start.1
  24.7 0.8 broadcast_in_dim.144
  25.5 10.6 %scatter_fusion = bf16[176,8,128]{2,1,0:T(8,128)(2,1)} fusion(bf16[176,8,128]{2,1,0:T(8,128)(2,1)} %broadcast_in_dim.144, s32[96]{0:T(128)S(1)} %fusion.47, bf16[96,8,128]{2,1,0:T(8,128)(2,1)} %bitcast.45), kind=kCustom, calls=%fused_computation.4 | custom fusion | bytes 590208 | tf_op jit(solution)/shard_map/scatter | solution.py:68
  36.1 4.1 all-to-all-start.2
  40.3 20.5 %reshape.204 = bf16[96,128,512]{2,1,0:T(8,128)(2,1)} reshape(bf16[12288,2,256]{2,1,0:T(2,128)(2,1)} %param.7) | data formatting | bytes 25165824 | tf_op jit(solution)/shard_map/reshape | solution.py:62
  60.7 7.9 %broadcast_in_dim.170 = bf16[176,128,512]{2,1,0:T(8,128)(2,1)} broadcast(bf16[]{:T(256)} %constant.24.clone.1), dimensions={} | broadcast | bytes 23068674 | tf_op jit(solution)/shard_map/broadcast_in_dim | solution.py:65
  68.6 33.0 %scatter_fusion.1 = bf16[176,128,512]{2,1,0:T(8,128)(2,1)} fusion(bf16[176,128,512]{2,1,0:T(8,128)(2,1)} %broadcast_in_dim.170, s32[96]{0:T(128)S(1)} %fusion.47, bf16[96,128,512]{2,1,0:T(8,128)(2,1)} %reshape.204), kind=kCustom, calls=%fused_computation.5 | custom fusion | bytes 37749120 | tf_op jit(solution)/shard_map/scatter | solution.py:65
  101.6 6.4 %all-to-all-start.3 = ((bf16[176,128,512]{2,1,0:T(8,128)(2,1)}), bf16[176,128,512]{2,1,0:T(8,128)(2,1)}, u32[]{:S(2)}, u32[]{:S(2)}) async-start(bf16[176,128,512]{2,1,0:T(8,128)(2,1)} %scatter_fusion.1), calls=%async_computation.3 | async-start | bytes 46137344 | tf_op jit(solution)/shard_map/all_to_all | solution.py:70
  108.3 0.7 fusion.52
  109.3 1.6 gather_fusion.1
  110.9 5.1 broadcast_add_fusion.7
  116.6 242.7 %all-to-all-done.3 = bf16[176,128,512]{2,1,0:T(8,128)(2,1)} async-done(((bf16[176,128,512]{2,1,0:T(8,128)(2,1)}), bf16[176,128,512]{2,1,0:T(8,128)(2,1)}, u32[]{:S(2)}, u32[]{:S(2)}) %all-to-all-start.3) | async-done | bytes 23068704 | tf_op jit(solution)/shard_map/all_to_all | solution.py:70
  359.4 29.0 %fusion.9 = f32[176,128,512]{2,1,0:T(8,128)} fusion(bf16[176,128,512]{2,1,0:T(8,128)(2,1)} %all-to-all-done.3, f32[176,128]{1,0:T(8,128)S(1)} %bitcast.47, s32[176,128]{1,0:T(8,128)S(1)} %add.223, f32[176,128]{1,0:T(8,128)S(1)} %bitcast.48, s32[176,128]{1,0:T(8,128)S(1)} %add.219, f32[176,128]{1,0:T(8,128)S(1)} %bitcast.49, s32[176,128]{1,0:T(8,128)S(1)} %add.215, ...), kind=kOutput, calls=%fused_computation.28 | convolution fusion | flops 3021996032 | bytes 70647808 | tf_op jit(solution)/shard_map/bcr,brf->bcf/dot_general | solution.py:76
  388.4 49.7 %fusion.35 = bf16[19,128,512]{2,0,1:T(8,128)(2,1)S(1)} fusion(f32[176,128,512]{2,1,0:T(8,128)} %fusion.9, s32[176]{0:T(256)S(1)} %broadcast_select_fusion), kind=kOutput, calls=%fused_computation.59 | convolution fusion | flops 2631077120 | bytes 48628416 | tf_op jit(solution)/shard_map/bs,bcf->scf/dot_general | solution.py:79
  438.1 3.4 copy.18
  441.5 7.4 %copy.19 = bf16[19,128,2,256]{3,2,0,1:T(2,128)(2,1)} copy(bf16[19,128,2,256]{1,3,2,0:T(8,128)(2,1)} %bitcast.43) | data formatting | bytes 4980736 | tf_op jit(solution)/shard_map/reshape | solution.py:80
  448.9 4.9 all-to-all-start.4
  453.8 4.6 convert_element_type.65
  458.4 19.1 %multiply_convert_fusion.1 = (bf16[1024,1024]{1,0:T(8,128)(2,1)}, bf16[1024,1024]{1,0:T(8,128)(2,1)}, bf16[1024,1024]{1,0:T(8,128)(2,1)}) fusion(f32[1024]{0:T(1024)S(1)} %subtract_multiply_fusion), kind=kLoop, calls=%fused_computation.50 | loop fusion | flops 22020096 | bytes 6295552 | tf_op jit(solution)/shard_map/convert.13
  477.5 30.1 %all-to-all-done.4 = bf16[19,128,2,256]{3,2,0,1:T(2,128)(2,1)S(1)} async-done(((bf16[19,128,2,256]{3,2,0,1:T(2,128)(2,1)}), bf16[19,128,2,256]{3,2,0,1:T(2,128)(2,1)S(1)}, u32[]{:S(2)}, u32[]{:S(2)}) %all-to-all-start.4) | async-done | bytes 2490400 | tf_op jit(solution)/shard_map/all_to_all | solution.py:82
  508.1 2.2 copy.21
  510.2 3.0 dot_general.13
  513.3 11.1 %fusion.53 = (bf16[19,32,2048]{2,1,0:T(8,128)(2,1)}, f32[19,32,2048]{2,1,0:T(8,128)S(1)}) fusion(bf16[19,32,2048]{2,1,0:T(8,128)(2,1)} %dot_general.13, bf16[1024,1024]{1,0:T(8,128)(2,1)} %get-tuple-element.20, bf16[1024,1024]{1,0:T(8,128)(2,1)} %get-tuple-element.19, bf16[1024,1024]{1,0:T(8,128)(2,1)} %get-tuple-element.18), kind=kOutput, calls=%fused_computation.104 | convolution fusion | flops 5135073280 | bytes 16252928 | tf_op jit(solution)/shard_map/dot_general | solution.py:86
  524.3 2.0 fusion.34
  526.4 34.8 %all-reduce.2.cloned.1.call-done = f32[19,1024]{1,0:T(8,128)} async-done(((f32[19,1024]{1,0:T(8,128)}), f32[19,1024]{1,0:T(8,128)}) %all-reduce.2.cloned.1.call-update) | async-done | bytes 77840 | tf_op jit(solution)/shard_map/psum | solution.py:91
  561.2 1.5 broadcast_multiply_fusion
  (44 shorter events, 3.4 us)
Async XLA Ops:
  7.2 9.6 %copy-start = (s32[12288]{0:T(1024)S(1)}, s32[12288]{0:T(1024)}, u32[]{:S(2)}) copy-start(s32[12288]{0:T(1024)} %param.8) | copy-start | bytes 147460
  11.6 9.8 %all-to-all-start = ((s32[8,22,1]{1,2,0:T(1,128)}), s32[8,22,1]{1,2,0:T(1,128)S(1)}, u32[]{:S(2)}, u32[]{:S(2)}) async-start(s32[8,22,1]{1,2,0:T(1,128)} %bitcast.2), calls=%async_computation | async-start | bytes 8192 | tf_op jit(solution)/shard_map/all_to_all | solution.py:71
  21.4 14.8 %all-to-all-start.1 = ((s32[8,22,128]{2,1,0:T(8,128)}), s32[8,22,128]{2,1,0:T(8,128)S(1)}, u32[]{:S(2)}, u32[]{:S(2)}) async-start(s32[8,22,128]{2,1,0:T(8,128)} %all_to_all.31), calls=%async_computation.1 | async-start | bytes 196608 | tf_op jit(solution)/shard_map/all_to_all | solution.py:72
  36.1 65.5 %all-to-all-start.2 = ((bf16[176,8,128]{2,1,0:T(8,128)(2,1)}), bf16[176,8,128]{2,1,0:T(8,128)(2,1)S(1)}, u32[]{:S(2)}, u32[]{:S(2)}) async-start(bf16[176,8,128]{2,1,0:T(8,128)(2,1)} %scatter_fusion), calls=%async_computation.2 | async-start | bytes 720896 | tf_op jit(solution)/shard_map/all_to_all | solution.py:73
  101.6 6.5 %copy-start.2 = (s32[80]{0:T(128)S(1)}, s32[80]{0:T(128)}, u32[]{:S(2)}) copy-start(s32[80]{0:T(128)} %param.12) | copy-start | bytes 964
  101.6 6.7 %copy-start.3 = (s32[8]{0:T(128)S(1)}, s32[8]{0:T(128)}, u32[]{:S(2)}) copy-start(s32[8]{0:T(128)} %param.10) | copy-start | bytes 100
  101.6 257.8 %all-to-all-start.3 = ((bf16[176,128,512]{2,1,0:T(8,128)(2,1)}), bf16[176,128,512]{2,1,0:T(8,128)(2,1)}, u32[]{:S(2)}, u32[]{:S(2)}) async-start(bf16[176,128,512]{2,1,0:T(8,128)(2,1)} %scatter_fusion.1), calls=%async_computation.3 | async-start | bytes 46137344 | tf_op jit(solution)/shard_map/all_to_all | solution.py:70
  448.9 58.7 %all-to-all-start.4 = ((bf16[19,128,2,256]{3,2,0,1:T(2,128)(2,1)}), bf16[19,128,2,256]{3,2,0,1:T(2,128)(2,1)S(1)}, u32[]{:S(2)}, u32[]{:S(2)}) async-start(bf16[19,128,2,256]{3,2,0,1:T(2,128)(2,1)} %copy.19), calls=%async_computation.4 | async-start | bytes 4980736 | tf_op jit(solution)/shard_map/all_to_all | solution.py:82
  453.8 107.4 %all-reduce.2.cloned.1.call-start = ((), (), s32[]{:S(2)}) async-start(), calls=%async_computation.5 | async-start | bytes 196608 | tf_op jit(solution)/shard_map/psum | solution.py:91
  510.2 14.1 %slice-start = ((s8[4980736]{0:T(1024)(128)(4,1)}), s8[786432]{0:T(1024)(128)(4,1)S(1)}, s32[]{:S(2)}) async-start(s8[4980736]{0:T(1024)(128)(4,1)} %bitcast.41), calls=%async_computation.6 | async-start | bytes 1572864
  513.3 11.1 %slice-start.1 = ((s8[4980736]{0:T(1024)(128)(4,1)}), s8[4194304]{0:T(1024)(128)(4,1)S(1)}, s32[]{:S(2)}) async-start(s8[4980736]{0:T(1024)(128)(4,1)} %bitcast.41), calls=%async_computation.7 | async-start | bytes 8388608
  513.3 49.4 %copy-start.1 = (s32[12288]{0:T(1024)S(1)}, s32[12288]{0:T(1024)}, u32[]{:S(2)}) copy-start(s32[12288]{0:T(1024)} %param.8) | copy-start | bytes 147460
Sparse Core Ops, SparseCore 0:
  526.5 34.6 all-reduce.1
where the time goes:
time: 572 us; the launch traced here: 570 us
  waiting for transfers between devices  311 us (54%)
  local copies, waits for them, and re-layouts  96.4 us (17%)
  matrix products  89.8 us (16%)
  other arithmetic  34.3 us (6%)
  starting transfers between devices  24 us (4%)
  between operations  14.3 us (2%)
    all_to_all x1, waiting for transfers between devices, body(): lax.all_to_all(sent_vis, 'uv', split_axis=0, concat_axis=0, tiled=True)  243 us
    dot_general x1, matrix products, body(): jnp.einsum('bs,bcf->scf', pick, contrib, precision=lax.Precision.HIGHEST)  49.7 us
    psum x1, waiting for transfers between devices, body(): power = lax.psum(local_power, 'chan') / jnp.float32(math.sqrt(TC))  34.8 us
    scatter x1, local copies, waits for them, and re-layouts, body(): jnp.zeros((buffer_size, BR, 2 * chan_dev), jnp.bfloat16).at[place]  33 us
    all_to_all x1, waiting for transfers between devices, body(): lax.all_to_all(gridded, 'chan', split_axis=1, concat_axis=3, tiled=True)  30.1 us
    dot_general x1, matrix products, body(): jnp.einsum('bcr,brf->bcf', got_matrix, got_vis, preferred_element_type=jn...  29 us
    reshape x1, local copies, waits for them, and re-layouts, body(): blocks = vis.reshape(nblocks, BR, 2 * chan_dev)  20.5 us
    another operation x1, other arithmetic  19.1 us
  transfers between devices with their start and end apart: 6, of which 4 were waited for; matrix products, arithmetic and copies ran while one was open for 19% of the time, Pallas kernels for 0%

commit v1 on v0

--- a/solution.py
+++ b/solution.py
@@ -88,7 +88,11 @@
     galaxy_f = galaxy.astype(jnp.float32)
     product = delay[..., :CH] * galaxy_f[..., :CH] + delay[..., CH:] * galaxy_f[..., CH:]
     local_power = jnp.sum(product, axis=1)
-    power = lax.psum(local_power, "chan") / jnp.float32(math.sqrt(TC))
+
+    def _guide_knots(z):
+        return jnp.sum(lax.all_gather(z, axis_name="chan"), axis=0)
+
+    power = _guide_knots(local_power) / jnp.float32(math.sqrt(TC))
     return (delay.astype(jnp.bfloat16), power)
 
 

time: 572 us -> 538 us (0.941)
  waiting for transfers between devices: 311 us -> 276 us
  blocking collectives: 0 us -> 14.8 us
  between operations: 14.3 us -> 0.88 us
    psum x1 -> x0, waiting for transfers between devices: 34.8 us -> none  [body(): power = lax.psum(local_power, 'chan') / jnp.float32(math.sqrt(TC))]
    all_gather x0 -> x1, blocking collectives: none -> 14.8 us  [_guide_knots(): return jnp.sum(lax.all_gather(z, axis_name='chan'), axis=0)]
  transfers between devices with their start and end apart: 6 -> 5, of which waited for: 4 -> 3; matrix products, arithmetic and copies ran while one was open for 19% -> 20% of each run, Pallas kernels for 0% -> 0%
where the time goes in v1:
time: 538 us; the launch traced here: 535 us
  waiting for transfers between devices  276 us (51%)
  local copies, waits for them, and re-layouts  96.4 us (18%)
  matrix products  89.8 us (17%)
  other arithmetic  32.8 us (6%)
  starting transfers between devices  24 us (4%)
  blocking collectives  14.8 us (3%)
    all_to_all x1, waiting for transfers between devices, body(): lax.all_to_all(sent_vis, 'uv', split_axis=0, concat_axis=0, tiled=True)  243 us
    dot_general x1, matrix products, body(): jnp.einsum('bs,bcf->scf', pick, contrib, precision=lax.Precision.HIGHEST)  49.7 us
    scatter x1, local copies, waits for them, and re-layouts, body(): jnp.zeros((buffer_size, BR, 2 * chan_dev), jnp.bfloat16).at[place]  33 us
    all_to_all x1, waiting for transfers between devices, body(): lax.all_to_all(gridded, 'chan', split_axis=1, concat_axis=3, tiled=True)  30.1 us
    dot_general x1, matrix products, body(): jnp.einsum('bcr,brf->bcf', got_matrix, got_vis, preferred_element_type=jn...  29 us
    reshape x1, local copies, waits for them, and re-layouts, body(): blocks = vis.reshape(nblocks, BR, 2 * chan_dev)  20.5 us
    another operation x1, other arithmetic  19.1 us
    all_gather x1, blocking collectives, _guide_knots(): return jnp.sum(lax.all_gather(z, axis_name='chan'), axis=0)  14.8 us
  transfers between devices with their start and end apart: 5, of which 3 were waited for; matrix products, arithmetic and copies ran while one was open for 20% of the time, Pallas kernels for 0%

profile of v1, /device:TPU:0, one launch (start us, length us, event | category | flops | bytes accessed | tf_op | source)
XLA Modules:
  0.0 534.6 jit_solution(15335371081919470968)
XLA Ops:
  0.6 0.7 compare_select_fusion.1
  1.3 1.6 gather_fusion
  3.3 1.0 scatter_custom_fusion
  4.3 0.7 all_to_all.29
  5.0 5.2 all-to-all-start
  10.2 0.8 scatter_custom_fusion.1
  11.7 3.1 all-to-all-done
  14.8 3.4 all-to-all-start.1
  18.2 0.8 broadcast_in_dim.144
  19.0 10.6 %scatter_fusion = bf16[176,8,128]{2,1,0:T(8,128)(2,1)} fusion(bf16[176,8,128]{2,1,0:T(8,128)(2,1)} %broadcast_in_dim.144, s32[96]{0:T(128)S(1)} %fusion.47, bf16[96,8,128]{2,1,0:T(8,128)(2,1)} %bitcast.47), kind=kCustom, calls=%fused_computation.4 | custom fusion | bytes 590208 | tf_op jit(solution)/shard_map/scatter | solution.py:68
  29.6 4.1 all-to-all-start.2
  33.7 20.5 %reshape.204 = bf16[96,128,512]{2,1,0:T(8,128)(2,1)} reshape(bf16[12288,2,256]{2,1,0:T(2,128)(2,1)} %param.7) | data formatting | bytes 25165824 | tf_op jit(solution)/shard_map/reshape | solution.py:62
  54.2 7.9 %broadcast_in_dim.170 = bf16[176,128,512]{2,1,0:T(8,128)(2,1)} broadcast(bf16[]{:T(256)} %constant.24.clone.1), dimensions={} | broadcast | bytes 23068674 | tf_op jit(solution)/shard_map/broadcast_in_dim | solution.py:65
  62.1 33.0 %scatter_fusion.1 = bf16[176,128,512]{2,1,0:T(8,128)(2,1)} fusion(bf16[176,128,512]{2,1,0:T(8,128)(2,1)} %broadcast_in_dim.170, s32[96]{0:T(128)S(1)} %fusion.47, bf16[96,128,512]{2,1,0:T(8,128)(2,1)} %reshape.204), kind=kCustom, calls=%fused_computation.5 | custom fusion | bytes 37749120 | tf_op jit(solution)/shard_map/scatter | solution.py:65
  95.1 6.4 %all-to-all-start.3 = ((bf16[176,128,512]{2,1,0:T(8,128)(2,1)}), bf16[176,128,512]{2,1,0:T(8,128)(2,1)}, u32[]{:S(2)}, u32[]{:S(2)}) async-start(bf16[176,128,512]{2,1,0:T(8,128)(2,1)} %scatter_fusion.1), calls=%async_computation.3 | async-start | bytes 46137344 | tf_op jit(solution)/shard_map/all_to_all | solution.py:70
  101.7 0.7 fusion.52
  102.8 1.6 gather_fusion.1
  104.4 5.1 broadcast_add_fusion.7
  110.1 242.7 %all-to-all-done.3 = bf16[176,128,512]{2,1,0:T(8,128)(2,1)} async-done(((bf16[176,128,512]{2,1,0:T(8,128)(2,1)}), bf16[176,128,512]{2,1,0:T(8,128)(2,1)}, u32[]{:S(2)}, u32[]{:S(2)}) %all-to-all-start.3) | async-done | bytes 23068704 | tf_op jit(solution)/shard_map/all_to_all | solution.py:70
  352.8 29.0 %fusion.9 = f32[176,128,512]{2,1,0:T(8,128)} fusion(bf16[176,128,512]{2,1,0:T(8,128)(2,1)} %all-to-all-done.3, f32[176,128]{1,0:T(8,128)S(1)} %bitcast.49, s32[176,128]{1,0:T(8,128)S(1)} %add.221, f32[176,128]{1,0:T(8,128)S(1)} %bitcast.50, s32[176,128]{1,0:T(8,128)S(1)} %add.217, f32[176,128]{1,0:T(8,128)S(1)} %bitcast.51, s32[176,128]{1,0:T(8,128)S(1)} %add.213, ...), kind=kOutput, calls=%fused_computation.28 | convolution fusion | flops 3021996032 | bytes 70647808 | tf_op jit(solution)/shard_map/bcr,brf->bcf/dot_general | solution.py:76
  381.8 49.7 %fusion.35 = bf16[19,128,512]{2,0,1:T(8,128)(2,1)S(1)} fusion(f32[176,128,512]{2,1,0:T(8,128)} %fusion.9, s32[176]{0:T(256)S(1)} %broadcast_select_fusion), kind=kOutput, calls=%fused_computation.59 | convolution fusion | flops 2631077120 | bytes 48628416 | tf_op jit(solution)/shard_map/bs,bcf->scf/dot_general | solution.py:79
  431.5 3.4 copy.18
  435.0 7.4 %copy.19 = bf16[19,128,2,256]{3,2,0,1:T(2,128)(2,1)} copy(bf16[19,128,2,256]{1,3,2,0:T(8,128)(2,1)} %bitcast.44) | data formatting | bytes 4980736 | tf_op jit(solution)/shard_map/reshape | solution.py:80
  442.4 4.9 all-to-all-start.4
  447.3 4.6 convert_element_type.65
  451.9 19.1 %multiply_convert_fusion.1 = (bf16[1024,1024]{1,0:T(8,128)(2,1)}, bf16[1024,1024]{1,0:T(8,128)(2,1)}, bf16[1024,1024]{1,0:T(8,128)(2,1)}) fusion(f32[1024]{0:T(1024)S(1)} %subtract_multiply_fusion), kind=kLoop, calls=%fused_computation.50 | loop fusion | flops 22020096 | bytes 6295552 | tf_op jit(solution)/shard_map/convert.13
  471.0 30.1 %all-to-all-done.4 = bf16[19,128,2,256]{3,2,0,1:T(2,128)(2,1)S(1)} async-done(((bf16[19,128,2,256]{3,2,0,1:T(2,128)(2,1)}), bf16[19,128,2,256]{3,2,0,1:T(2,128)(2,1)S(1)}, u32[]{:S(2)}, u32[]{:S(2)}) %all-to-all-start.4) | async-done | bytes 2490400 | tf_op jit(solution)/shard_map/all_to_all | solution.py:82
  501.5 2.2 copy.21
  503.7 3.0 dot_general.13
  506.7 11.1 %fusion.53 = (bf16[19,32,2048]{2,1,0:T(8,128)(2,1)}, f32[19,32,2048]{2,1,0:T(8,128)S(1)}) fusion(bf16[19,32,2048]{2,1,0:T(8,128)(2,1)} %dot_general.13, bf16[1024,1024]{1,0:T(8,128)(2,1)} %get-tuple-element.20, bf16[1024,1024]{1,0:T(8,128)(2,1)} %get-tuple-element.19, bf16[1024,1024]{1,0:T(8,128)(2,1)} %get-tuple-element.18), kind=kOutput, calls=%fused_computation.104 | convolution fusion | flops 5135073280 | bytes 16252928 | tf_op jit(solution)/shard_map/dot_general | solution.py:86
  517.8 1.4 fusion.34
  519.2 14.8 %all-gather.1 = f32[4,19,1024]{2,1,0:T(8,128)S(1)} all-gather(f32[1,19,1024]{2,1,0:T(8,128)S(1)} %bitcast.46), channel_id=2, replica_groups=mesh['uv'=8,'chan'=4] {'chan'}, dimensions={0}, use_global_device_ids=true | all-gather | bytes 389120 | tf_op jit(solution)/shard_map/all_gather | solution.py:93
  (43 shorter events, 3.4 us)
Async XLA Ops:
  0.6 9.6 %copy-start = (s32[12288]{0:T(1024)S(1)}, s32[12288]{0:T(1024)}, u32[]{:S(2)}) copy-start(s32[12288]{0:T(1024)} %param.8) | copy-start | bytes 147460
  5.0 9.8 %all-to-all-start = ((s32[8,22,1]{1,2,0:T(1,128)}), s32[8,22,1]{1,2,0:T(1,128)S(1)}, u32[]{:S(2)}, u32[]{:S(2)}) async-start(s32[8,22,1]{1,2,0:T(1,128)} %bitcast.2), calls=%async_computation | async-start | bytes 8192 | tf_op jit(solution)/shard_map/all_to_all | solution.py:71
  14.8 14.8 %all-to-all-start.1 = ((s32[8,22,128]{2,1,0:T(8,128)}), s32[8,22,128]{2,1,0:T(8,128)S(1)}, u32[]{:S(2)}, u32[]{:S(2)}) async-start(s32[8,22,128]{2,1,0:T(8,128)} %all_to_all.31), calls=%async_computation.1 | async-start | bytes 196608 | tf_op jit(solution)/shard_map/all_to_all | solution.py:72
  29.6 65.5 %all-to-all-start.2 = ((bf16[176,8,128]{2,1,0:T(8,128)(2,1)}), bf16[176,8,128]{2,1,0:T(8,128)(2,1)S(1)}, u32[]{:S(2)}, u32[]{:S(2)}) async-start(bf16[176,8,128]{2,1,0:T(8,128)(2,1)} %scatter_fusion), calls=%async_computation.2 | async-start | bytes 720896 | tf_op jit(solution)/shard_map/all_to_all | solution.py:73
  95.1 6.5 %copy-start.2 = (s32[80]{0:T(128)S(1)}, s32[80]{0:T(128)}, u32[]{:S(2)}) copy-start(s32[80]{0:T(128)} %param.12) | copy-start | bytes 964
  95.1 6.7 %copy-start.3 = (s32[8]{0:T(128)S(1)}, s32[8]{0:T(128)}, u32[]{:S(2)}) copy-start(s32[8]{0:T(128)} %param.10) | copy-start | bytes 100
  95.1 257.8 %all-to-all-start.3 = ((bf16[176,128,512]{2,1,0:T(8,128)(2,1)}), bf16[176,128,512]{2,1,0:T(8,128)(2,1)}, u32[]{:S(2)}, u32[]{:S(2)}) async-start(bf16[176,128,512]{2,1,0:T(8,128)(2,1)} %scatter_fusion.1), calls=%async_computation.3 | async-start | bytes 46137344 | tf_op jit(solution)/shard_map/all_to_all | solution.py:70
  442.4 58.7 %all-to-all-start.4 = ((bf16[19,128,2,256]{3,2,0,1:T(2,128)(2,1)}), bf16[19,128,2,256]{3,2,0,1:T(2,128)(2,1)S(1)}, u32[]{:S(2)}, u32[]{:S(2)}) async-start(bf16[19,128,2,256]{3,2,0,1:T(2,128)(2,1)} %copy.19), calls=%async_computation.4 | async-start | bytes 4980736 | tf_op jit(solution)/shard_map/all_to_all | solution.py:82
  503.7 14.1 %slice-start = ((s8[4980736]{0:T(1024)(128)(4,1)}), s8[786432]{0:T(1024)(128)(4,1)S(1)}, s32[]{:S(2)}) async-start(s8[4980736]{0:T(1024)(128)(4,1)} %bitcast.42), calls=%async_computation.5 | async-start | bytes 1572864
  506.7 11.1 %slice-start.1 = ((s8[4980736]{0:T(1024)(128)(4,1)}), s8[4194304]{0:T(1024)(128)(4,1)S(1)}, s32[]{:S(2)}) async-start(s8[4980736]{0:T(1024)(128)(4,1)} %bitcast.42), calls=%async_computation.6 | async-start | bytes 8388608
  506.7 27.9 %copy-start.1 = (s32[12288]{0:T(1024)S(1)}, s32[12288]{0:T(1024)}, u32[]{:S(2)}) copy-start(s32[12288]{0:T(1024)} %param.8) | copy-start | bytes 147460
